TPU v7x, 128 devices: a whole 4x4x4 slice. The times are simulated.
128 devices in a mesh: ex: 8 (over z, core), sh: 16 (over y, x).
Axes of the slice: x: 4, y: 4, z: 4, core: 2. Of those that a mesh axis runs over, the one named last changes fastest.
Arguments:
- hidden_in: bfloat16 [12288, 2304], P(('ex', 'sh')), may hold values from -3 to 3
- queries: bfloat16 [12288, 2304], P(('ex', 'sh')), may hold values from -2.5 to 2.5
- new_keys: bfloat16 [12288, 2304], P(('ex', 'sh')), may hold values from -2.5 to 2.5
- new_values: bfloat16 [12288, 2304], P(('ex', 'sh')), may hold values from -6 to 6
- key_pool: bfloat16 [131072, 2304], P(('ex', 'sh')), may hold values from -2.5 to 2.5
- value_pool: bfloat16 [131072, 2304], P(('ex', 'sh')), may hold values from -6 to 6
- page_order: int32 [128, 64], P(('ex', 'sh')), may hold values from 0 to 63, each once within a row
- new_lengths: int32 [128, 4], P(('ex', 'sh')), may hold values from 1 to 48, 96 in all within a row
- context_lengths: int32 [128, 4], P(('ex', 'sh')), may hold values from 1 to 256, 512 in all within a row
- route_ids: int32 [12288, 2], P(('ex', 'sh')), may hold values from 0 to 7, all different within a row; in each aligned block of 96 rows (0 to 95, 96 to 191, ...) at most 32 rows name the same one
- norm_gain: bfloat16 [2304], replicated, may hold values from 0.25 to 1.75
- router_weight: bfloat16 [2304, 8], replicated, may hold values from -0.125 to 0.125
- gate_weight: bfloat16 [8, 2304, 5760], P('ex', None, 'sh'), may hold values from -0.125 to 0.125
- up_weight: bfloat16 [8, 2304, 5760], P('ex', None, 'sh'), may hold values from -0.125 to 0.125
- down_weight: bfloat16 [8, 5760, 2304], P('ex', 'sh'), may hold values from -0.078125 to 0.078125
- out_gain: bfloat16 [2304], replicated, may hold values from 0.25 to 1.75
Outputs:
- layer_out: bfloat16 [12288, 2304], P(('ex', 'sh'))
Inputs may be any that keep to these rules, and one draw needn't show every extreme that they name: `page_order`: each row names the pages 0 to 63 of one device's pool once each; request r owns entries r * 16 to (r+1) * 16 - 1 of its row, in order. `new_lengths`: each row sums to 96; its largest entry is 48. `context_lengths`: each row sums to 512; its largest entry is 256. `route_ids`: A row names two different experts. Among the 96 rows of one device no expert is named by more than 32 rows, and in some devices' rows one expert is named by exactly 32.
All inputs are finite; a program needn't handle non-finite values.
Results may differ from a plain program's by a relative error of at most 0.015.
Values may be sent and summed in bfloat16 or wider, within the bound.
No kernel may reach another device: no remote copies, remote signals or barrier semaphores. Data moves between devices by JAX's collectives and lax.ppermute only.
A program may use at most 128 MiB of HBM per device.

v0:
```python
import jax
import jax.numpy as jnp
from jax import lax
from jax.sharding import PartitionSpec as P

HEADS = 36
HEAD_DIM = 64
EXPERTS = 8
PAGE = 16
MOST = 32
CTX_TOTAL = 512


def rms_scale(values, gain):
    mean_square = jnp.mean(values * values, axis=-1, keepdims=True)
    return values * lax.rsqrt(mean_square + 1e-05) * gain.astype(jnp.float32)


def route_probs(normed, router_weight, route_ids):
    logits = jnp.dot(normed, router_weight, preferred_element_type=jnp.float32)
    expert_range = jnp.arange(router_weight.shape[1], dtype=jnp.int32)
    picked = jnp.sum(
        jnp.where(route_ids[:, :, None] == expert_range[None, None, :], logits[:, None, :], 0.0),
        axis=2,
    )
    raised = jnp.exp(picked)
    return raised / jnp.sum(raised, axis=1, keepdims=True)


def attend(
    hidden_rows,
    query_rows,
    key_rows,
    value_rows,
    key_store,
    value_store,
    page_row,
    new_row_lengths,
    context_row_lengths,
):
    row_count = query_rows.shape[0]
    requests = new_row_lengths.shape[0]
    table = page_row.reshape(requests, -1)
    ends = jnp.cumsum(new_row_lengths)
    row_index = jnp.arange(row_count, dtype=jnp.int32)
    owner = jnp.sum((row_index[:, None] >= ends[None, :]).astype(jnp.int32), axis=1)
    context_ends = jnp.cumsum(context_row_lengths)
    slot = jnp.arange(CTX_TOTAL, dtype=jnp.int32)
    slot_owner = jnp.sum((slot[:, None] >= context_ends[None, :]).astype(jnp.int32), axis=1)
    position = slot - (context_ends - context_row_lengths)[slot_owner]
    token = table[slot_owner, position // PAGE] * PAGE + position % PAGE
    key_store = key_store[token]
    value_store = value_store[token]
    store_mask = owner[:, None] == slot_owner[None, :]
    fresh_mask = (owner[:, None] == owner[None, :]) & (row_index[None, :] <= row_index[:, None])
    allowed = jnp.concatenate([store_mask, fresh_mask], axis=1)
    keys = jnp.concatenate([key_store, key_rows], axis=0).reshape(-1, HEADS, HEAD_DIM)
    values = jnp.concatenate([value_store, value_rows], axis=0).reshape(-1, HEADS, HEAD_DIM)
    query_heads = query_rows.reshape(row_count, HEADS, HEAD_DIM)
    scores = jnp.einsum(
        "rhd,khd->hrk", query_heads, keys, preferred_element_type=jnp.float32
    ) * HEAD_DIM ** (-0.5)
    raised = jnp.where(allowed[None, :, :], jnp.exp(scores), 0.0)
    weights = (raised / jnp.sum(raised, axis=2, keepdims=True)).astype(jnp.bfloat16)
    attended = jnp.einsum(
        "hrk,khd->rhd", weights, values, preferred_element_type=jnp.float32
    ).reshape(row_count, HEADS * HEAD_DIM)
    return hidden_rows.astype(jnp.float32) + attended


def per_device(
    hidden_in,
    queries,
    new_keys,
    new_values,
    key_pool,
    value_pool,
    page_order,
    new_lengths,
    context_lengths,
    route_ids,
    norm_gain,
    router_weight,
    gate_weight,
    up_weight,
    down_weight,
    out_gain,
):
    groups = lax.axis_size("ex")
    local_experts = gate_weight.shape[0]
    width = hidden_in.shape[1]
    row_count = hidden_in.shape[0]
    resid = attend(
        hidden_in,
        queries,
        new_keys,
        new_values,
        key_pool,
        value_pool,
        page_order[0],
        new_lengths[0],
        context_lengths[0],
    )
    normed = rms_scale(resid, norm_gain).astype(jnp.bfloat16)
    route_weights = route_probs(normed, router_weight, route_ids)
    top_count = route_ids.shape[1]
    entries = route_ids.reshape(-1)
    expert_range = jnp.arange(EXPERTS, dtype=jnp.int32)
    onehot = (entries[:, None] == expert_range[None, :]).astype(jnp.int32)
    before = jnp.cumsum(onehot, axis=0) - onehot
    slot_index = jnp.sum(before * onehot, axis=1)
    target = entries * MOST + slot_index
    entry_rows = jnp.arange(entries.shape[0], dtype=jnp.int32) // top_count
    source_row = jnp.zeros((EXPERTS * MOST,), jnp.int32).at[target].set(entry_rows)
    filled = jnp.zeros((EXPERTS * MOST,), jnp.bool_).at[target].set(True)
    outgoing = jnp.where(filled[:, None], normed[source_row], jnp.zeros((), jnp.bfloat16)).reshape(
        EXPERTS, MOST, width
    )
    arrived = lax.all_to_all(outgoing, "ex", split_axis=0, concat_axis=0, tiled=True).reshape(
        groups * MOST, width
    )
    arrived_rows = lax.all_gather(arrived, "sh", axis=0, tiled=True)
    gate_value = jnp.dot(arrived_rows, gate_weight[0], preferred_element_type=jnp.float32)
    up_value = jnp.dot(arrived_rows, up_weight[0], preferred_element_type=jnp.float32)
    hidden = (jax.nn.silu(gate_value) * up_value).astype(jnp.bfloat16)
    partial = jnp.dot(hidden, down_weight[0], preferred_element_type=jnp.float32).astype(
        jnp.bfloat16
    )
    summed = lax.psum_scatter(partial, "sh", scatter_dimension=0, tiled=True)
    returned = lax.all_to_all(
        summed.reshape(EXPERTS, MOST, width), "ex", split_axis=0, concat_axis=0, tiled=True
    )
    flat_results = returned.reshape(EXPERTS * MOST, width)
    picked = flat_results[target].reshape(row_count, top_count, width)
    mixed = resid + jnp.sum(route_weights[:, :, None] * picked.astype(jnp.float32), axis=1)
    return rms_scale(mixed, out_gain).astype(jnp.bfloat16)


def solution(mesh):
    placed = (
        P(("ex", "sh"), None),
        P(("ex", "sh"), None),
        P(("ex", "sh"), None),
        P(("ex", "sh"), None),
        P(("ex", "sh"), None),
        P(("ex", "sh"), None),
        P(("ex", "sh"), None),
        P(("ex", "sh"), None),
        P(("ex", "sh"), None),
        P(("ex", "sh"), None),
        P(),
        P(),
        P("ex", None, "sh"),
        P("ex", None, "sh"),
        P("ex", "sh", None),
        P(),
    )
    return jax.shard_map(
        per_device, mesh=mesh, in_specs=placed, out_specs=P(("ex", "sh"), None), check_vma=False
    )
```

profile of v0, /device:TPU:1, one launch (start us, length us, event | category | flops | bytes accessed | tf_op | source)
XLA Modules:
  0.0 417.7 jit_solution(15909731302938036896)
XLA Ops:
  6.5 0.8 broadcast_multiply_fusion.1
  7.4 0.8 copy.37
  8.2 0.8 reduce-window.26
  9.6 0.8 reduce-window.27
  11.1 1.3 reduce.5
  13.4 2.6 fusion.17
  16.0 4.8 %gather_fusion = s32[512]{0:T(512)S(1)} fusion(s32[4,16]{1,0:T(4,128)S(1)} %reshape_squeeze.3, s32[512]{0:T(512)S(1)} %bitcast.61), kind=kCustom, calls=%fused_computation | custom fusion | bytes 8192 | tf_op jit(solution)/shard_map/gather | solution.py:51
  20.8 0.7 convert_element_type.44
  22.9 1.2 scatter_custom_fusion.1
  24.1 1.4 scatter_custom_fusion
  26.0 8.8 %gather_fusion.2 = bf16[512,2304]{1,0:T(8,128)(2,1)} fusion(bf16[1024,2304]{1,0:T(8,128)(2,1)} %param.20, s32[1024]{0:T(1024)S(1)} %pad_clamp_fusion.2), kind=kCustom, calls=%fused_computation.2 | custom fusion | bytes 4720640 | tf_op jit(solution)/shard_map/gather | solution.py:52
  34.7 3.4 pad_maximum_fusion.1
  38.2 5.4 %copy.32 = bf16[608,2304]{0,1:T(8,128)(2,1)} copy(bf16[608,2304]{1,0:T(8,128)(2,1)} %pad_maximum_fusion.1) | data formatting | bytes 5603328 | tf_op jit(solution)/shard_map/concatenate | solution.py:57
  43.6 8.7 %gather_fusion.1 = bf16[512,2304]{1,0:T(8,128)(2,1)} fusion(bf16[1024,2304]{1,0:T(8,128)(2,1)} %param.21, s32[1024]{0:T(1024)S(1)} %pad_clamp_fusion.2), kind=kCustom, calls=%fused_computation.1 | custom fusion | bytes 4720640 | tf_op jit(solution)/shard_map/gather | solution.py:53
  52.3 3.4 pad_maximum_fusion
  55.7 5.4 %copy.31 = bf16[608,2304]{0,1:T(8,128)(2,1)} copy(bf16[608,2304]{1,0:T(8,128)(2,1)} %pad_maximum_fusion) | data formatting | bytes 5603328 | tf_op jit(solution)/shard_map/concatenate | solution.py:58
  61.2 4.2 %fusion = (f32[36,96]{1,0:T(8,128)S(1)}, f32[36,608,96]{1,2,0:T(8,128)S(1)}) fusion(pred[96,608]{1,0:T(8,128)(4,1)S(1)} %pad_add_fusion, bf16[608,36,64]{0,2,1:T(8,128)(2,1)} %bitcast.64, bf16[96,36,64]{0,2,1:T(8,128)(2,1)S(1)} %bitcast.68), kind=kOutput, calls=%fused_computation.10 | convolution fusion | flops 275260032 | bytes 11721216 | tf_op jit(solution)/shard_map/rhd,khd->hrk/dot_general | solution.py:60
  65.4 3.5 fusion.2
  68.9 1.6 copy.34
  71.0 2.4 gather_fusion.3
  73.4 1.4 broadcast_select_fusion
  74.8 23.2 %all_to_all.10 = bf16[8,32,2304]{2,1,0:T(8,128)(2,1)} all-to-all(bf16[8,32,2304]{2,1,0:T(8,128)(2,1)S(1)} %broadcast_select_fusion), channel_id=1, replica_groups=mesh['ex'=8,'sh'=16] {'ex'}, dimensions={0} | all-to-all | bytes 2359296 | tf_op jit(solution)/shard_map/all_to_all | solution.py:119
  98.4 121.2 %all-gather.2.cloned.1.call-done = bf16[4096,2304]{1,0:T(8,128)(2,1)} async-done(((bf16[256,2304]{1,0:T(8,128)(2,1)}), bf16[4096,2304]{1,0:T(8,128)(2,1)}) %all-gather.2.cloned.1.call-update) | async-done | bytes 18874384 | tf_op jit(solution)/shard_map/all_gather | solution.py:122
  219.6 13.0 %fusion.7 = f32[4096,360]{0,1:T(8,128)} fusion(bf16[4096,2304]{1,0:T(8,128)(2,1)} %all-gather.2.cloned.1.call-done, bf16[1,2304,360]{1,2,0:T(8,128)(2,1)} %param.28), kind=kOutput, calls=%fused_computation.19 | convolution fusion | flops 6794772480 | bytes 26431488 | tf_op jit(solution)/shard_map/dot_general | solution.py:123
  232.6 25.2 %convolution_convert_fusion = bf16[4096,2304]{1,0:T(8,128)(2,1)} fusion(bf16[1,360,2304]{2,1,0:T(8,128)(2,1)S(1)} %copy-done, bf16[4096,2304]{1,0:T(8,128)(2,1)} %all-gather.2.cloned.1.call-done, f32[4096,360]{0,1:T(8,128)} %fusion.7, bf16[1,2304,360]{1,2,0:T(8,128)(2,1)} %param.29), kind=kOutput, calls=%fused_computation.7 | convolution fusion | flops 13607829504 | bytes 46964736 | tf_op jit(solution)/shard_map/dot_general | solution.py:126
  257.8 120.5 %reduce-scatter.2.cloned.1.call-done = bf16[256,2304]{1,0:T(8,128)(2,1)} async-done(((bf16[4096,2304]{1,0:T(8,128)(2,1)}), bf16[256,2304]{1,0:T(8,128)(2,1)}) %reduce-scatter.2.cloned.1.call-update) | async-done | bytes 1179664 | tf_op jit(solution)/shard_map/reduce_scatter | solution.py:129
  378.3 5.6 %all-to-all-start.1 = ((bf16[8,32,2304]{2,1,0:T(8,128)(2,1)}), bf16[8,32,2304]{2,1,0:T(8,128)(2,1)S(1)}, u32[]{:S(2)}, u32[]{:S(2)}) async-start(bf16[8,32,2304]{2,1,0:T(8,128)(2,1)} %bitcast.66), calls=%async_computation.2 | async-start | bytes 2359296 | tf_op jit(solution)/shard_map/all_to_all | solution.py:130
  384.3 15.9 %all-to-all-done.1 = bf16[8,32,2304]{2,1,0:T(8,128)(2,1)S(1)} async-done(((bf16[8,32,2304]{2,1,0:T(8,128)(2,1)}), bf16[8,32,2304]{2,1,0:T(8,128)(2,1)S(1)}, u32[]{:S(2)}, u32[]{:S(2)}) %all-to-all-start.1) | async-done | bytes 1179680 | tf_op jit(solution)/shard_map/all_to_all | solution.py:130
  400.2 2.1 gather_fusion.4
  402.4 3.3 reshape.302
  405.6 4.0 multiply_reduce_fusion
  409.9 1.0 multiply_convert_fusion
  (70 shorter events, 5.5 us)
Async XLA Ops:
  6.5 226.0 %copy-start = (bf16[1,360,2304]{2,1,0:T(8,128)(2,1)S(1)}, bf16[1,360,2304]{2,1,0:T(8,128)(2,1)}, u32[]{:S(2)}) copy-start(bf16[1,360,2304]{2,1,0:T(8,128)(2,1)} %param.30) | copy-start | bytes 4976644
  6.5 19.1 %copy-start.6 = (bf16[96,2304]{1,0:T(8,128)(2,1)S(1)}, bf16[96,2304]{1,0:T(8,128)(2,1)}, u32[]{:S(2)}) copy-start(bf16[96,2304]{1,0:T(8,128)(2,1)} %param.17) | copy-start | bytes 1327108
  6.5 213.0 %all-gather.2.cloned.1.call-start = ((), (), s32[]{:S(2)}) async-start(), calls=%async_computation.3 | async-start | bytes 20054016 | tf_op jit(solution)/shard_map/all_gather | solution.py:122
  25.9 8.8 %copy-start.7 = (bf16[96,2304]{1,0:T(8,128)(2,1)S(1)}, bf16[96,2304]{1,0:T(8,128)(2,1)}, u32[]{:S(2)}) copy-start(bf16[96,2304]{1,0:T(8,128)(2,1)} %param.18) | copy-start | bytes 1327108
  43.6 8.7 %copy-start.8 = (bf16[96,2304]{1,0:T(8,128)(2,1)S(1)}, bf16[96,2304]{1,0:T(8,128)(2,1)}, u32[]{:S(2)}) copy-start(bf16[96,2304]{1,0:T(8,128)(2,1)} %param.19) | copy-start | bytes 1327108
  61.2 4.2 %copy-start.5 = (bf16[608,2304]{0,1:T(8,128)(2,1)S(1)}, bf16[608,2304]{0,1:T(8,128)(2,1)}, u32[]{:S(2)}) copy-start(bf16[608,2304]{0,1:T(8,128)(2,1)} %copy.31) | copy-start | bytes 8404996
  65.4 5.1 %copy-start.3 = (bf16[96,2304]{1,0:T(8,128)(2,1)S(1)}, bf16[96,2304]{1,0:T(8,128)(2,1)}, u32[]{:S(2)}) copy-start(bf16[96,2304]{1,0:T(8,128)(2,1)} %param.16) | copy-start | bytes 1327108
  70.6 2.8 copy-start.1
  98.1 280.2 %reduce-scatter.2.cloned.1.call-start = ((), (), s32[]{:S(2)}) async-start(), calls=%async_computation.4 | async-start | bytes 20054016 | tf_op jit(solution)/shard_map/reduce_scatter | solution.py:129
  257.8 126.1 %copy-start.11 = (bf16[2304]{0:T(1024)(128)(2,1)S(1)}, bf16[2304]{0:T(1024)(128)(2,1)}, u32[]{:S(2)}) copy-start(bf16[2304]{0:T(1024)(128)(2,1)} %param.31) | copy-start | bytes 13828
  257.8 126.1 %copy-start.9 = (bf16[2304,8]{0,1:T(8,128)(2,1)S(1)}, bf16[2304,8]{0,1:T(8,128)(2,1)}, u32[]{:S(2)}) copy-start(bf16[2304,8]{0,1:T(8,128)(2,1)} %param.27) | copy-start | bytes 110596
  257.8 126.3 %copy-start.10 = (s32[96,2]{0,1:T(2,128)S(1)}, s32[96,2]{0,1:T(2,128)}, u32[]{:S(2)}) copy-start(s32[96,2]{0,1:T(2,128)} %param.25) | copy-start | bytes 2308
  378.3 21.9 %all-to-all-start.1 = ((bf16[8,32,2304]{2,1,0:T(8,128)(2,1)}), bf16[8,32,2304]{2,1,0:T(8,128)(2,1)S(1)}, u32[]{:S(2)}, u32[]{:S(2)}) async-start(bf16[8,32,2304]{2,1,0:T(8,128)(2,1)} %bitcast.66), calls=%async_computation.2 | async-start | bytes 2359296 | tf_op jit(solution)/shard_map/all_to_all | solution.py:130
  402.4 7.3 %copy-start.2 = (f32[96,2304]{1,0:T(8,128)S(1)}, f32[96,2304]{1,0:T(8,128)}, u32[]{:S(2)}) copy-start(f32[96,2304]{1,0:T(8,128)} %copy-done.1) | copy-start | bytes 2654212
  402.4 7.3 %copy-start.4 = (bf16[96,2304]{1,0:T(8,128)(2,1)S(1)}, bf16[96,2304]{1,0:T(8,128)(2,1)}, u32[]{:S(2)}) copy-start(bf16[96,2304]{1,0:T(8,128)(2,1)} %param.16) | copy-start | bytes 1327108
Sparse Core Ops, SparseCore 0:
  98.2 121.3 all-gather.1
  257.9 120.3 reduce-scatter.1
where the time goes:
time: 418 us
  waiting for transfers between devices  258 us (62%)
  local copies, waits for them, and re-layouts  48.4 us (12%)
  matrix products  46.1 us (11%)
  blocking collectives  23.2 us (6%)
  other arithmetic  22.9 us (5%)
  between operations  13.7 us (3%)
  starting transfers between devices  5.84 us (1%)
    all_gather x1, waiting for transfers between devices, per_device(): arrived_rows = lax.all_gather(arrived, 'sh', axis=0, tiled=True)  121 us
    reduce_scatter x1, waiting for transfers between devices, per_device(): summed = lax.psum_scatter(partial, 'sh', scatter_dimension=0, tiled=True)  121 us
    dot_general x1, matrix products, per_device(): jnp.dot(hidden, down_weight[0], preferred_element_type=jnp.float32)  25.2 us
    all_to_all x1, blocking collectives, per_device(): lax.all_to_all(outgoing, 'ex', split_axis=0, concat_axis=0, tiled=True)  23.2 us
    all_to_all x1, waiting for transfers between devices, per_device(): lax.all_to_all(summed.reshape(EXPERTS, MOST, width), 'ex', split_axis=0,...  15.9 us
    dot_general x1, matrix products, per_device(): jnp.dot(arrived_rows, gate_weight[0], preferred_element_type=jnp.float32)  13 us
    gather x1, local copies, waits for them, and re-layouts, attend(): key_store = key_store[token]  8.78 us
    gather x1, local copies, waits for them, and re-layouts, attend(): value_store = value_store[token]  8.73 us
  transfers between devices with their start and end apart: 3, of which 3 were waited for; matrix products, arithmetic and copies ran while one was open for 0% of the time, Pallas kernels for 0%

commit v1 on v0

--- a/solution.py
+++ b/solution.py
@@ -9,6 +9,21 @@
 PAGE = 16
 MOST = 32
 CTX_TOTAL = 512
+
+
+def produce_trees(u, axis_k, vec):
+    main, back = (u.shape[:axis_k], u.shape[axis_k + 1 :])
+    g_now = jnp.moveaxis(u.reshape(*main, vec, -1, *back), axis_k, 0)
+    return g_now
+
+
+def state_weights(original, array_axis):
+    original = jnp.moveaxis(original, 0, array_axis)
+    outer = original.shape
+    x_new = original.reshape(
+        *outer[:array_axis], outer[array_axis] * outer[array_axis + 1], *outer[array_axis + 2 :]
+    )
+    return x_new
 
 
 def rms_scale(values, gain):
@@ -127,9 +142,21 @@
         jnp.bfloat16
     )
     summed = lax.psum_scatter(partial, "sh", scatter_dimension=0, tiled=True)
-    returned = lax.all_to_all(
-        summed.reshape(EXPERTS, MOST, width), "ex", split_axis=0, concat_axis=0, tiled=True
-    )
+
+    def link_the_indices(matrix, comm_axis, x_local, local):
+        top, shaped = (lax.psum(1, comm_axis), lax.axis_index(comm_axis))
+        carry = produce_trees(matrix, x_local, top)
+        history = [carry[shaped]]
+        for no in range(1, top):
+            local_out = carry[shaped ^ no]
+            history.append(
+                lax.ppermute(local_out, comm_axis, [(dev_j, dev_j ^ no) for dev_j in range(top)])
+            )
+        carry = jnp.stack(history, axis=0)[shaped ^ jnp.arange(top)]
+        t1 = state_weights(carry, local)
+        return t1
+
+    returned = link_the_indices(summed.reshape(EXPERTS, MOST, width), "ex", 0, 0)
     flat_results = returned.reshape(EXPERTS * MOST, width)
     picked = flat_results[target].reshape(row_count, top_count, width)
     mixed = resid + jnp.sum(route_weights[:, :, None] * picked.astype(jnp.float32), axis=1)

time: 418 us -> 425 us (1.017)
  local copies, waits for them, and re-layouts: 48.4 us -> 55 us
    all_to_all x1 -> x0, waiting for transfers between devices: 15.9 us -> none  [per_device(): lax.all_to_all(summed.reshape(EXPERTS, MOST, width), 'ex', split_axis=0,...]
    ppermute x0 -> x7, waiting for transfers between devices: none -> 15.3 us  [link_the_indices(): lax.ppermute(local_out, comm_axis, [(dev_j, dev_j ^ no) for dev_j in rang...]
    ppermute x0 -> x7, starting transfers between devices: none -> 7.87 us  [link_the_indices(): lax.ppermute(local_out, comm_axis, [(dev_j, dev_j ^ no) for dev_j in rang...]
    all_to_all x1 -> x0, starting transfers between devices: 5.57 us -> none  [per_device(): lax.all_to_all(summed.reshape(EXPERTS, MOST, width), 'ex', split_axis=0,...]
  transfers between devices with their start and end apart: 3 -> 9, of which waited for: 3 -> 4; matrix products, arithmetic and copies ran while one was open for 0% -> 0% of each run, Pallas kernels for 0% -> 0%
where the time goes in v1:
time: 425 us
  waiting for transfers between devices  256 us (60%)
  local copies, waits for them, and re-layouts  55 us (13%)
  matrix products  46.1 us (11%)
  blocking collectives  23.2 us (5%)
  other arithmetic  22.3 us (5%)
  between operations  13.8 us (3%)
  starting transfers between devices  8.14 us (2%)
    all_gather x1, waiting for transfers between devices, per_device(): arrived_rows = lax.all_gather(arrived, 'sh', axis=0, tiled=True)  121 us
    reduce_scatter x1, waiting for transfers between devices, per_device(): summed = lax.psum_scatter(partial, 'sh', scatter_dimension=0, tiled=True)  120 us
    dot_general x1, matrix products, per_device(): jnp.dot(hidden, down_weight[0], preferred_element_type=jnp.float32)  25.2 us
    all_to_all x1, blocking collectives, per_device(): lax.all_to_all(outgoing, 'ex', split_axis=0, concat_axis=0, tiled=True)  23.2 us
    ppermute x7, waiting for transfers between devices, link_the_indices(): lax.ppermute(local_out, comm_axis, [(dev_j, dev_j ^ no) for dev_j in rang...  15.3 us
    dot_general x1, matrix products, per_device(): jnp.dot(arrived_rows, gate_weight[0], preferred_element_type=jnp.float32)  13 us
    gather x1, local copies, waits for them, and re-layouts, attend(): key_store = key_store[token]  8.78 us
    gather x1, local copies, waits for them, and re-layouts, attend(): value_store = value_store[token]  8.73 us
  transfers between devices with their start and end apart: 9, of which 4 were waited for; matrix products, arithmetic and copies ran while one was open for 0% of the time, Pallas kernels for 0%

profile of v1, /device:TPU:1, one launch (start us, length us, event | category | flops | bytes accessed | tf_op | source)
XLA Modules:
  0.0 424.6 jit_solution(11209382772405830494)
XLA Ops:
  11.1 1.3 reduce.5
  13.4 2.6 fusion.17
  16.0 4.8 %gather_fusion = s32[512]{0:T(512)S(1)} fusion(s32[4,16]{1,0:T(4,128)S(1)} %reshape_squeeze.3, s32[512]{0:T(512)S(1)} %bitcast.92), kind=kCustom, calls=%fused_computation | custom fusion | bytes 8192 | tf_op jit(solution)/shard_map/gather | solution.py:66
  22.2 1.2 scatter_custom_fusion.1
  23.4 1.4 scatter_custom_fusion
  25.3 8.8 %gather_fusion.2 = bf16[512,2304]{1,0:T(8,128)(2,1)} fusion(bf16[1024,2304]{1,0:T(8,128)(2,1)} %param.20, s32[1024]{0:T(1024)S(1)} %pad_clamp_fusion.3), kind=kCustom, calls=%fused_computation.2 | custom fusion | bytes 4720640 | tf_op jit(solution)/shard_map/gather | solution.py:67
  34.1 3.4 pad_maximum_fusion.1
  37.5 5.4 %copy.32 = bf16[608,2304]{0,1:T(8,128)(2,1)} copy(bf16[608,2304]{1,0:T(8,128)(2,1)} %pad_maximum_fusion.1) | data formatting | bytes 5603328 | tf_op jit(solution)/shard_map/concatenate | solution.py:72
  42.9 8.7 %gather_fusion.1 = bf16[512,2304]{1,0:T(8,128)(2,1)} fusion(bf16[1024,2304]{1,0:T(8,128)(2,1)} %param.21, s32[1024]{0:T(1024)S(1)} %pad_clamp_fusion.3), kind=kCustom, calls=%fused_computation.1 | custom fusion | bytes 4720640 | tf_op jit(solution)/shard_map/gather | solution.py:68
  51.6 3.4 pad_maximum_fusion
  55.1 5.4 %copy.31 = bf16[608,2304]{0,1:T(8,128)(2,1)} copy(bf16[608,2304]{1,0:T(8,128)(2,1)} %pad_maximum_fusion) | data formatting | bytes 5603328 | tf_op jit(solution)/shard_map/concatenate | solution.py:73
  60.5 4.2 fusion
  64.8 3.5 fusion.2
  68.3 1.7 copy.34
  70.3 2.4 gather_fusion.3
  72.8 1.4 broadcast_select_fusion
  74.2 23.2 %all_to_all.5 = bf16[8,32,2304]{2,1,0:T(8,128)(2,1)} all-to-all(bf16[8,32,2304]{2,1,0:T(8,128)(2,1)S(1)} %broadcast_select_fusion), channel_id=1, replica_groups=mesh['ex'=8,'sh'=16] {'ex'}, dimensions={0} | all-to-all | bytes 2359296 | tf_op jit(solution)/shard_map/all_to_all | solution.py:134
  97.7 121.2 %all-gather.2.cloned.1.call-done = bf16[4096,2304]{1,0:T(8,128)(2,1)} async-done(((bf16[256,2304]{1,0:T(8,128)(2,1)}), bf16[4096,2304]{1,0:T(8,128)(2,1)}) %all-gather.2.cloned.1.call-update) | async-done | bytes 18874384 | tf_op jit(solution)/shard_map/all_gather | solution.py:137
  218.9 13.0 %fusion.7 = f32[4096,360]{0,1:T(8,128)} fusion(bf16[4096,2304]{1,0:T(8,128)(2,1)} %all-gather.2.cloned.1.call-done, bf16[1,2304,360]{1,2,0:T(8,128)(2,1)} %param.28), kind=kOutput, calls=%fused_computation.20 | convolution fusion | flops 6794772480 | bytes 26431488 | tf_op jit(solution)/shard_map/dot_general | solution.py:138
  231.9 25.2 %convolution_convert_fusion = bf16[4096,2304]{1,0:T(8,128)(2,1)} fusion(bf16[1,360,2304]{2,1,0:T(8,128)(2,1)S(1)} %copy-done, bf16[4096,2304]{1,0:T(8,128)(2,1)} %all-gather.2.cloned.1.call-done, f32[4096,360]{0,1:T(8,128)} %fusion.7, bf16[1,2304,360]{1,2,0:T(8,128)(2,1)} %param.29), kind=kOutput, calls=%fused_computation.8 | convolution fusion | flops 13607829504 | bytes 46964736 | tf_op jit(solution)/shard_map/dot_general | solution.py:141
  258.2 119.5 %reduce-scatter.2.cloned.1.call-done = bf16[256,2304]{1,0:T(8,128)(2,1)} async-done(((bf16[4096,2304]{1,0:T(8,128)(2,1)}), bf16[256,2304]{1,0:T(8,128)(2,1)}) %reduce-scatter.2.cloned.1.call-update) | async-done | bytes 1179664 | tf_op jit(solution)/shard_map/reduce_scatter | solution.py:144
  377.7 2.1 dynamic-slice_bitcast_fusion
  379.8 1.1 collective-permute-start
  381.1 2.6 collective-permute-start.6
  383.9 2.2 collective-permute-start.4
  386.1 1.3 collective-permute-start.3
  388.6 9.7 %collective-permute-done.1 = bf16[1,32,2304]{2,1,0:T(8,128)(2,1)S(1)} collective-permute-done((bf16[1,32,2304]{2,1,0:T(8,128)(2,1)}, bf16[1,32,2304]{2,1,0:T(8,128)(2,1)S(1)}, u32[]{:S(2)}, u32[]{:S(2)}) %collective-permute-start.1) | collective-permute-done | bytes 147488 | tf_op jit(solution)/shard_map/ppermute | solution.py:153
  398.4 5.7 %collective-permute-done.2 = bf16[1,32,2304]{2,1,0:T(8,128)(2,1)S(1)} collective-permute-done((bf16[1,32,2304]{2,1,0:T(8,128)(2,1)S(1)}, bf16[1,32,2304]{2,1,0:T(8,128)(2,1)S(1)}, u32[]{:S(2)}, u32[]{:S(2)}) %collective-permute-start.2) | collective-permute-done | bytes 147488 | tf_op jit(solution)/shard_map/ppermute | solution.py:153
  405.2 1.9 gather_fusion.4
  407.1 2.1 gather_fusion.5
  409.3 3.2 reshape.310
  412.4 4.1 multiply_reduce_fusion
  (92 shorter events, 13.0 us)
Async XLA Ops:
  6.5 225.4 %copy-start = (bf16[1,360,2304]{2,1,0:T(8,128)(2,1)S(1)}, bf16[1,360,2304]{2,1,0:T(8,128)(2,1)}, u32[]{:S(2)}) copy-start(bf16[1,360,2304]{2,1,0:T(8,128)(2,1)} %param.30) | copy-start | bytes 4976644
  6.5 14.3 %copy-start.10 = (bf16[2304]{0:T(1024)(128)(2,1)S(1)}, bf16[2304]{0:T(1024)(128)(2,1)}, u32[]{:S(2)}) copy-start(bf16[2304]{0:T(1024)(128)(2,1)} %param.26) | copy-start | bytes 13828
  6.5 18.4 %copy-start.5 = (bf16[96,2304]{1,0:T(8,128)(2,1)S(1)}, bf16[96,2304]{1,0:T(8,128)(2,1)}, u32[]{:S(2)}) copy-start(bf16[96,2304]{1,0:T(8,128)(2,1)} %param.17) | copy-start | bytes 1327108
  6.5 212.4 %all-gather.2.cloned.1.call-start = ((), (), s32[]{:S(2)}) async-start(), calls=%async_computation.2 | async-start | bytes 20054016 | tf_op jit(solution)/shard_map/all_gather | solution.py:137
  25.3 8.8 %copy-start.6 = (bf16[96,2304]{1,0:T(8,128)(2,1)S(1)}, bf16[96,2304]{1,0:T(8,128)(2,1)}, u32[]{:S(2)}) copy-start(bf16[96,2304]{1,0:T(8,128)(2,1)} %param.18) | copy-start | bytes 1327108
  42.9 8.7 %copy-start.7 = (bf16[96,2304]{1,0:T(8,128)(2,1)S(1)}, bf16[96,2304]{1,0:T(8,128)(2,1)}, u32[]{:S(2)}) copy-start(bf16[96,2304]{1,0:T(8,128)(2,1)} %param.19) | copy-start | bytes 1327108
  60.5 4.2 copy-start.3
  68.3 1.7 copy-start.2
  97.5 280.2 %reduce-scatter.2.cloned.1.call-start = ((), (), s32[]{:S(2)}) async-start(), calls=%async_computation.3 | async-start | bytes 20054016 | tf_op jit(solution)/shard_map/reduce_scatter | solution.py:144
  257.1 0.8 copy-start.8
  257.1 1.0 copy-start.9
  257.1 123.8 %copy-start.11 = (bf16[2304]{0:T(1024)(128)(2,1)S(1)}, bf16[2304]{0:T(1024)(128)(2,1)}, u32[]{:S(2)}) copy-start(bf16[2304]{0:T(1024)(128)(2,1)} %param.31) | copy-start | bytes 13828
  379.8 7.6 %collective-permute-start = (bf16[1,32,2304]{2,1,0:T(8,128)(2,1)}, bf16[1,32,2304]{2,1,0:T(8,128)(2,1)}, u32[]{:S(2)}, u32[]{:S(2)}) collective-permute-start(bf16[1,32,2304]{2,1,0:T(8,128)(2,1)} %get-tuple-element.13), channel_id=1, source_target_pairs={{0,16},{16,0},{32,48},{48,32},{64,80},{80,64},{96,112},{112,96},{1... | collective-permute-start | bytes 442376 | tf_op jit(solution)/shard_map/ppermute | solution.py:153
  381.1 23.1 %collective-permute-start.6 = (bf16[1,32,2304]{2,1,0:T(8,128)(2,1)S(1)}, bf16[1,32,2304]{2,1,0:T(8,128)(2,1)S(1)}, u32[]{:S(2)}, u32[]{:S(2)}) collective-permute-start(bf16[1,32,2304]{2,1,0:T(8,128)(2,1)S(1)} %get-tuple-element.7), channel_id=1, source_target_pairs={{0,112},{16,96},{32,80},{48,64},{64,48},{80,32},{96,16},{112,0},{1... | collective-permute-start | bytes 442376 | tf_op jit(solution)/shard_map/ppermute | solution.py:153
  383.7 20.4 %collective-permute-start.5 = (bf16[1,32,2304]{2,1,0:T(8,128)(2,1)S(1)}, bf16[1,32,2304]{2,1,0:T(8,128)(2,1)S(1)}, u32[]{:S(2)}, u32[]{:S(2)}) collective-permute-start(bf16[1,32,2304]{2,1,0:T(8,128)(2,1)S(1)} %get-tuple-element.8), channel_id=1, source_target_pairs={{0,96},{16,112},{32,64},{48,80},{64,32},{80,48},{96,0},{112,16},{1... | collective-permute-start | bytes 442376 | tf_op jit(solution)/shard_map/ppermute | solution.py:153
  383.9 20.2 %collective-permute-start.4 = (bf16[1,32,2304]{2,1,0:T(8,128)(2,1)S(1)}, bf16[1,32,2304]{2,1,0:T(8,128)(2,1)S(1)}, u32[]{:S(2)}, u32[]{:S(2)}) collective-permute-start(bf16[1,32,2304]{2,1,0:T(8,128)(2,1)S(1)} %get-tuple-element.9), channel_id=1, source_target_pairs={{0,80},{16,64},{32,112},{48,96},{64,16},{80,0},{96,48},{112,32},{1... | collective-permute-start | bytes 442376 | tf_op jit(solution)/shard_map/ppermute | solution.py:153
  386.1 18.0 %collective-permute-start.3 = (bf16[1,32,2304]{2,1,0:T(8,128)(2,1)S(1)}, bf16[1,32,2304]{2,1,0:T(8,128)(2,1)S(1)}, u32[]{:S(2)}, u32[]{:S(2)}) collective-permute-start(bf16[1,32,2304]{2,1,0:T(8,128)(2,1)S(1)} %get-tuple-element.10), channel_id=1, source_target_pairs={{0,64},{16,80},{32,96},{48,112},{64,0},{80,16},{96,32},{112,48},{1... | collective-permute-start | bytes 442376 | tf_op jit(solution)/shard_map/ppermute | solution.py:153
  387.4 10.9 %collective-permute-start.1 = (bf16[1,32,2304]{2,1,0:T(8,128)(2,1)}, bf16[1,32,2304]{2,1,0:T(8,128)(2,1)S(1)}, u32[]{:S(2)}, u32[]{:S(2)}) collective-permute-start(bf16[1,32,2304]{2,1,0:T(8,128)(2,1)} %get-tuple-element.12), channel_id=1, source_target_pairs={{0,32},{16,48},{32,0},{48,16},{64,96},{80,112},{96,64},{112,80},{1... | collective-permute-start | bytes 442376 | tf_op jit(solution)/shard_map/ppermute | solution.py:153
  398.2 5.9 %collective-permute-start.2 = (bf16[1,32,2304]{2,1,0:T(8,128)(2,1)S(1)}, bf16[1,32,2304]{2,1,0:T(8,128)(2,1)S(1)}, u32[]{:S(2)}, u32[]{:S(2)}) collective-permute-start(bf16[1,32,2304]{2,1,0:T(8,128)(2,1)S(1)} %get-tuple-element.11), channel_id=1, source_target_pairs={{0,48},{16,32},{32,16},{48,0},{64,112},{80,96},{96,80},{112,64},{1... | collective-permute-start | bytes 442376 | tf_op jit(solution)/shard_map/ppermute | solution.py:153
  404.2 1.0 copy-start.4
  412.4 5.4 %copy-start.1 = (bf16[1,360,2304]{2,1,0:T(8,128)(2,1)S(1)}, bf16[1,360,2304]{2,1,0:T(8,128)(2,1)}, u32[]{:S(2)}) copy-start(bf16[1,360,2304]{2,1,0:T(8,128)(2,1)} %param.30) | copy-start | bytes 4976644
Sparse Core Ops, SparseCore 0:
  97.6 121.3 all-gather.1
  257.3 120.3 reduce-scatter.1
